TPU v7x, 512 devices: a whole 4x8x8 slice. The times are simulated.
512 devices in a mesh: dp: 16 (over y, core), expert: 32 (over x, z).
Axes of the slice: x: 4, y: 8, z: 8, core: 2. Of those that a mesh axis runs over, the one named last changes fastest.
Arguments:
- tokens: bfloat16 [65536, 1024], P(('dp', 'expert')), may hold values from -6 to 6
- routes: int32 [65536, 4], P(('dp', 'expert')), may hold values from 0 to 31, all different within a row; in each aligned block of 128 rows (0 to 127, 128 to 255, ...) at most 32 rows name the same one
- gates: float32 [65536, 4], P(('dp', 'expert')), may hold values from 0.05 to 0.5
- w_in: bfloat16 [32, 1024, 768], P('expert', 'dp'), may hold values from -6 to 6
- w_down: bfloat16 [32, 384, 1024], P('expert', 'dp'), may hold values from -6 to 6
- out_grad: bfloat16 [65536, 1024], P(('dp', 'expert')), may hold values from -6 to 6
Outputs:
- moe_out: bfloat16 [65536, 1024], P(('dp', 'expert'))
- token_grad: bfloat16 [65536, 1024], P(('dp', 'expert'))
- new_w_in: bfloat16 [32, 1024, 768], P('expert', 'dp')
- new_w_down: bfloat16 [32, 384, 1024], P('expert', 'dp')
Inputs may be any that keep to these rules, and one draw needn't show every extreme that they name: `routes`: within one device's 128 tokens no expert is named more than 32 times, a bound that some block reaches; a token names 4 different experts.
All inputs are finite; a program needn't handle non-finite values.
Results may differ from a plain program's by a relative error of at most 0.014.
Values may be sent and summed in bfloat16 or wider, within the bound.
No kernel may reach another device: no remote copies, remote signals or barrier semaphores. Data moves between devices by JAX's collectives and lax.ppermute only.
A program may use at most 64 MiB of HBM per device.

v0:
```python
import jax
import jax.numpy as jnp
from jax import lax
from jax.sharding import PartitionSpec as P

step_rate = 0.5


def slot_numbers(route_rows, experts, capacity):
    flat_routes = route_rows.reshape(-1)
    one_hot = (flat_routes[:, None] == jnp.arange(experts, dtype=jnp.int32)[None, :]).astype(
        jnp.int32
    )
    running = jnp.cumsum(one_hot, axis=0)
    position = jnp.sum(one_hot * running, axis=1) - 1
    return flat_routes * capacity + position


def expert_forward(inputs, full_in, full_down):
    model_width = full_in.shape[1]
    hidden_units = full_down.shape[1]
    projected = jnp.einsum(
        "sxcd,xdj->sxcj", inputs, full_in, preferred_element_type=jnp.float32
    ) * model_width ** (-0.5)
    gate_part = projected[..., :hidden_units]
    up_part = projected[..., hidden_units:]
    activation = (jax.nn.silu(gate_part) * up_part).astype(jnp.bfloat16)
    results = (
        jnp.einsum("sxcf,xfd->sxcd", activation, full_down, preferred_element_type=jnp.float32)
        * hidden_units ** (-0.5)
    ).astype(jnp.bfloat16)
    return (projected, activation, results)


def expert_backward(projected, grad_rows, full_in, full_down):
    model_width = full_in.shape[1]
    hidden_units = full_down.shape[1]
    grad_act = jnp.einsum(
        "sxcd,xfd->sxcf", grad_rows, full_down, preferred_element_type=jnp.float32
    ) * hidden_units ** (-0.5)
    gate_part = projected[..., :hidden_units]
    up_part = projected[..., hidden_units:]
    sigmoid_gate = jax.nn.sigmoid(gate_part)
    grad_gate = grad_act * up_part * sigmoid_gate * (1.0 + gate_part * (1.0 - sigmoid_gate))
    grad_up = grad_act * jax.nn.silu(gate_part)
    grad_hidden = jnp.concatenate([grad_gate, grad_up], axis=-1).astype(jnp.bfloat16)
    grad_inputs = (
        jnp.einsum("sxcj,xdj->sxcd", grad_hidden, full_in, preferred_element_type=jnp.float32)
        * model_width ** (-0.5)
    ).astype(jnp.bfloat16)
    return (grad_hidden, grad_inputs)


def body(tokens, routes, gates, w_in, w_down, out_grad):
    tok_rows, model_width = tokens.shape
    top_count = routes.shape[1]
    per_device = w_in.shape[0]
    hidden_units = w_down.shape[2] and w_in.shape[2] // 2
    sources = lax.axis_size("expert")
    experts = per_device * sources
    capacity = min(tok_rows, 2 * tok_rows * top_count // experts)
    slot_index = slot_numbers(routes, experts, capacity)
    token_of = jnp.arange(tok_rows * top_count, dtype=jnp.int32) // top_count
    layout = (sources, per_device, capacity, model_width)
    send_inputs = (
        jnp.zeros((experts * capacity, model_width), jnp.bfloat16)
        .at[slot_index]
        .set(tokens[token_of])
        .reshape(layout)
    )
    scaled = (gates.reshape(-1)[:, None] * out_grad[token_of].astype(jnp.float32)).astype(
        jnp.bfloat16
    )
    send_grads = (
        jnp.zeros((experts * capacity, model_width), jnp.bfloat16)
        .at[slot_index]
        .set(scaled)
        .reshape(layout)
    )
    full_in, full_down = (
        lax.all_gather(w_in, "dp", axis=1, tiled=True),
        lax.all_gather(w_down, "dp", axis=1, tiled=True),
    )
    inputs_here = lax.all_to_all(send_inputs, "expert", split_axis=0, concat_axis=0, tiled=True)
    projected_here, activation_here, results_here = expert_forward(inputs_here, full_in, full_down)
    results_home = lax.all_to_all(results_here, "expert", split_axis=0, concat_axis=0, tiled=True)
    grad_rows = lax.all_to_all(send_grads, "expert", split_axis=0, concat_axis=0, tiled=True)
    grad_hidden, grad_inputs = expert_backward(projected_here, grad_rows, full_in, full_down)
    inputs_back = lax.all_to_all(grad_inputs, "expert", split_axis=0, concat_axis=0, tiled=True)
    picked = results_home.reshape(experts * capacity, model_width)[slot_index].astype(jnp.float32)
    picked = picked.reshape(tok_rows, top_count, model_width)
    moe_out = jnp.sum(picked * gates[:, :, None], axis=1).astype(jnp.bfloat16)
    back_rows = inputs_back.reshape(experts * capacity, model_width)[slot_index].astype(jnp.float32)
    token_grad = jnp.sum(back_rows.reshape(tok_rows, top_count, model_width), axis=1).astype(
        jnp.bfloat16
    )
    column_part = inputs_here
    summed_in = lax.psum_scatter(
        (
            jnp.einsum(
                "sxcd,sxcj->dxj", column_part, grad_hidden, preferred_element_type=jnp.float32
            )
            * model_width ** (-0.5)
        ).astype(jnp.bfloat16),
        "dp",
        scatter_dimension=0,
        tiled=True,
    ).astype(jnp.float32)
    column_part = activation_here
    summed_down = lax.psum_scatter(
        (
            jnp.einsum("sxcf,sxcd->fxd", column_part, grad_rows, preferred_element_type=jnp.float32)
            * hidden_units ** (-0.5)
        ).astype(jnp.bfloat16),
        "dp",
        scatter_dimension=0,
        tiled=True,
    ).astype(jnp.float32)
    new_w_in = (w_in.astype(jnp.float32) - step_rate * jnp.transpose(summed_in, (1, 0, 2))).astype(
        jnp.bfloat16
    )
    new_w_down = (
        w_down.astype(jnp.float32) - step_rate * jnp.transpose(summed_down, (1, 0, 2))
    ).astype(jnp.bfloat16)
    return (moe_out, token_grad, new_w_in, new_w_down)


def solution(mesh):
    return jax.shard_map(
        body,
        mesh=mesh,
        in_specs=(
            P(("dp", "expert"), None),
            P(("dp", "expert"), None),
            P(("dp", "expert"), None),
            P("expert", "dp", None),
            P("expert", "dp", None),
            P(("dp", "expert"), None),
        ),
        out_specs=(
            P(("dp", "expert"), None),
            P(("dp", "expert"), None),
            P("expert", "dp", None),
            P("expert", "dp", None),
        ),
        check_vma=False,
    )
```

profile of v0, /device:TPU:25, one launch (start us, length us, event | category | flops | bytes accessed | tf_op | source)
XLA Modules:
  0.0 371.1 jit_solution(6107741425047522396)
XLA Ops:
  7.2 0.0 copy-start
  7.2 0.8 copy.34
  8.0 0.1 eq.29
  8.1 0.1 eq.25
  8.2 0.7 broadcast_multiply_fusion
  8.9 1.2 reduce-window.6
  10.1 0.2 slice_reduce_fusion
  10.4 0.1 fusion.51
  10.5 0.1 copy.33
  10.6 0.1 mul.160
  10.7 0.0 copy-done
  10.8 7.7 %scatter_custom_fusion = bf16[1024,1024]{1,0:T(8,128)(2,1)} fusion(s32[512]{0:T(512)S(1)} %bitcast.146, bf16[128,1024]{1,0:T(8,128)(2,1)S(1)} %copy-done, s32[1024]{0:T(1024)S(1)} %pad_clamp_fusion.1, bf16[]{:T(256)} %constant.17.clone.1), kind=kCustom, calls=%fused_computation.41 | custom fusion | bytes 2097154 | tf_op jit(solution)/shard_map/scatter | solution.py:68
  18.5 0.0 copy-start.5
  18.5 13.2 %all-to-all-start = ((bf16[32,1,32,1024]{3,2,1,0:T(8,128)(2,1)}), bf16[32,1,32,1024]{3,2,1,0:T(8,128)(2,1)S(1)}, u32[]{:S(2)}, u32[]{:S(2)}) async-start(bf16[32,1,32,1024]{3,2,1,0:T(8,128)(2,1)} %bitcast.4), calls=%async_computation | async-start | bytes 4194304 | tf_op jit(solution)/shard_map/all_to_all | solution.py:84
  31.7 0.0 copy-done.5
  31.7 0.1 copy.38
  31.8 0.1 mul.173
  31.9 0.0 copy-done.3
  32.0 7.8 %scatter_custom_fusion.1 = bf16[1024,1024]{1,0:T(8,128)(2,1)} fusion(s32[512]{0:T(512)S(1)} %bitcast.147, f32[512]{0:T(512)S(1)} %mul.173, bf16[]{:T(256)} %constant.17.clone.1, bf16[128,1024]{1,0:T(8,128)(2,1)S(1)} %copy-done.3, s32[1024]{0:T(1024)S(1)} %pad_clamp_fusion.1), kind=kCustom, calls=%fused_computation.40 | custom fusion | flops 1572864 | bytes 2365442 | tf_op jit(solution)/shard_map/scatter | solution.py:77
  39.8 40.7 %all-to-all-done = bf16[32,1,32,1024]{3,2,1,0:T(8,128)(2,1)S(1)} async-done(((bf16[32,1,32,1024]{3,2,1,0:T(8,128)(2,1)}), bf16[32,1,32,1024]{3,2,1,0:T(8,128)(2,1)S(1)}, u32[]{:S(2)}, u32[]{:S(2)}) %all-to-all-start) | async-done | bytes 2097184 | tf_op jit(solution)/shard_map/all_to_all | solution.py:84
  80.4 7.3 %all-to-all-start.2 = ((bf16[32,1,32,1024]{3,2,1,0:T(8,128)(2,1)}), bf16[32,1,32,1024]{3,2,1,0:T(8,128)(2,1)}, u32[]{:S(2)}, u32[]{:S(2)}) async-start(bf16[32,1,32,1024]{3,2,1,0:T(8,128)(2,1)} %bitcast.21), calls=%async_computation.2 | async-start | bytes 4194304 | tf_op jit(solution)/shard_map/all_to_all | solution.py:87
  87.7 0.0 all-gather.2.cloned.1.call-start
  87.8 0.7 all-gather.2.cloned.1.call-update
  88.4 0.0 copy-done.4
  88.4 18.9 %all_gather.7 = bf16[1,384,1024]{2,1,0:T(8,128)(2,1)S(1)} all-gather(bf16[1,24,1024]{2,1,0:T(8,128)(2,1)S(1)} %copy-done.4), channel_id=1, replica_groups=mesh['dp'=16,'expert'=32] {'dp'}, dimensions={1}, use_global_device_ids=true | all-gather | bytes 835584 | tf_op jit(solution)/shard_map/all_gather | solution.py:82
  107.4 26.6 %all-gather.2.cloned.1.call-done = bf16[1,1024,768]{2,1,0:T(8,128)(2,1)} async-done(((bf16[1,64,768]{2,1,0:T(8,128)(2,1)}), bf16[1,1024,768]{2,1,0:T(8,128)(2,1)}) %all-gather.2.cloned.1.call-update) | async-done | bytes 1572880 | tf_op jit(solution)/shard_map/all_gather | solution.py:81
  133.9 0.0 copy-done.1
  133.9 4.9 %multiply_bitcast_fusion = f32[32,1,32,768]{3,2,0,1:T(8,128)} fusion(bf16[32,1,32,1024]{3,2,1,0:T(8,128)(2,1)S(1)} %all-to-all-done, bf16[1,1024,768]{2,1,0:T(8,128)(2,1)} %all-gather.2.cloned.1.call-done), kind=kOutput, calls=%fused_computation.10 | convolution fusion | flops 1611399168 | bytes 6815744 | tf_op jit(solution)/shard_map/sxcd,xdj->sxcj/dot_general | solution.py:22
  138.9 0.0 all-to-all-done.2
  138.9 5.3 %fusion.44 = (bf16[32,32,384]{2,1,0:T(8,128)(2,1)S(1)}, bf16[32,32,384]{2,1,0:T(8,128)(2,1)S(1)}, bf16[32,32,384]{2,1,0:T(8,128)(2,1)}) fusion(f32[32,1,32,768]{3,2,0,1:T(8,128)} %multiply_bitcast_fusion, bf16[1,384,1024]{2,1,0:T(8,128)(2,1)S(1)} %all_gather.7, bf16[32,1,32,1024]{3,2,1,0:T(8,128)(2,1)} %all-to-all-done.2), kind=kOutput, calls=%fused_computation.50 | convolution fusion | flops 811597824 | bytes 8388608 | tf_op jit(solution)/shard_map/sxcd,xfd->sxcf/dot_general | solution.py:38
  144.2 0.9 copy-done.7
  145.1 0.2 copy-done.9
  145.4 0.0 copy-done.6
  145.4 3.2 fusion.14
  148.6 9.7 %all-to-all-start.3 = ((bf16[32,1,32,1024]{3,2,1,0:T(8,128)(2,1)}), bf16[32,1,32,1024]{3,2,1,0:T(8,128)(2,1)S(1)}, u32[]{:S(2)}, u32[]{:S(2)}) async-start(bf16[32,1,32,1024]{3,2,1,0:T(8,128)(2,1)} %fusion.14), calls=%async_computation.3 | async-start | bytes 4194304 | tf_op jit(solution)/shard_map/all_to_all | solution.py:89
  158.2 0.0 all-reduce.3.cloned.1.call-start
  158.3 3.9 %fusion.31 = bf16[384,1,1024]{0,2,1:T(8,128)(2,1)} fusion(bf16[32,32,384]{2,1,0:T(8,128)(2,1)} %get-tuple-element.18, bf16[32,1,32,1024]{3,2,1,0:T(8,128)(2,1)} %all-to-all-done.2), kind=kOutput, calls=%fused_computation.39 | convolution fusion | flops 806092800 | bytes 3670016 | tf_op jit(solution)/shard_map/sxcf,sxcd->fxd/dot_general | solution.py:112
  162.2 4.8 %copy.43 = bf16[384,1,1024]{2,1,0:T(2,128)(2,1)} copy(bf16[384,1,1024]{0,2,1:T(8,128)(2,1)} %fusion.31) | data formatting | bytes 1572864 | tf_op jit(solution)/shard_map/convert_element_type | solution.py:114
  167.0 0.0 all-reduce.3.cloned.1.call-update
  167.1 3.7 fusion.13
  170.8 36.4 %all-to-all-done.3 = bf16[32,1,32,1024]{3,2,1,0:T(8,128)(2,1)S(1)} async-done(((bf16[32,1,32,1024]{3,2,1,0:T(8,128)(2,1)}), bf16[32,1,32,1024]{3,2,1,0:T(8,128)(2,1)S(1)}, u32[]{:S(2)}, u32[]{:S(2)}) %all-to-all-start.3) | async-done | bytes 2097184 | tf_op jit(solution)/shard_map/all_to_all | solution.py:89
  207.1 7.6 %all-to-all-start.1 = ((bf16[32,1,32,1024]{3,2,1,0:T(8,128)(2,1)}), bf16[32,1,32,1024]{3,2,1,0:T(8,128)(2,1)}, u32[]{:S(2)}, u32[]{:S(2)}) async-start(bf16[32,1,32,1024]{3,2,1,0:T(8,128)(2,1)} %fusion.13), calls=%async_computation.1 | async-start | bytes 4194304 | tf_op jit(solution)/shard_map/all_to_all | solution.py:86
  214.8 0.0 reduce-scatter.4.cloned.1.call-start
  214.8 0.0 copy-done.8
  214.8 4.8 %fusion.23 = bf16[1024,768]{0,1:T(8,128)(2,1)} fusion(bf16[32,1,32,1024]{3,2,1,0:T(8,128)(2,1)} %copy-done.1, bf16[32,32,384]{2,1,0:T(8,128)(2,1)} %copy-done.9, bf16[32,32,384]{2,1,0:T(8,128)(2,1)S(1)} %copy-done.8), kind=kOutput, calls=%fused_computation.37 | convolution fusion | flops 1615331328 | bytes 5242880 | tf_op jit(solution)/shard_map/sxcd,sxcj->dxj/dot_general | solution.py:100
  219.7 2.6 copy.48
  222.3 0.0 reduce-scatter.4.cloned.1.call-update
  222.3 0.0 copy-done.2
  222.3 0.2 copy.41
  222.5 1.3 dynamic-slice
  224.5 62.4 %all-reduce.3.cloned.1.call-done = bf16[384,1,1024]{2,1,0:T(2,128)(2,1)} async-done(((bf16[384,1,1024]{2,1,0:T(2,128)(2,1)}), bf16[384,1,1024]{2,1,0:T(2,128)(2,1)}) %all-reduce.3.cloned.1.call-update) | async-done | bytes 786448
  286.8 1.0 fusion.49
  287.8 0.6 copy.45
  288.5 62.2 %reduce-scatter.4.cloned.1.call-done = bf16[64,768]{1,0:T(8,128)(2,1)} async-done(((bf16[1024,768]{1,0:T(8,128)(2,1)}), bf16[64,768]{1,0:T(8,128)(2,1)}) %reduce-scatter.4.cloned.1.call-update) | async-done | bytes 98320
  350.7 1.1 copy.49
  351.7 0.1 fusion.45
  351.8 0.8 copy.44
  352.6 2.0 gather_fusion.1
  354.6 0.4 gather.18
  355.1 2.1 reduce_sum.32
  357.2 0.0 all-to-all-done.1
  357.2 4.6 %gather_fusion = bf16[512,1024]{1,0:T(8,128)(2,1)S(1)} fusion(bf16[1024,1024]{1,0:T(8,128)(2,1)} %bitcast.20, s32[1024]{0:T(1024)S(1)} %pad_clamp_fusion), kind=kCustom, calls=%fused_computation.1 | custom fusion | bytes 2099200 | tf_op jit(solution)/shard_map/gather | solution.py:90
  361.8 0.7 reshape.219
  362.5 2.1 multiply_reduce_fusion
  (16 shorter events, 0.1 us)
Async XLA Ops:
  7.2 3.6 copy-start
  18.5 13.2 %copy-start.5 = (f32[128,4]{0,1:T(4,128)S(1)}, f32[128,4]{0,1:T(4,128)}, u32[]{:S(2)}) copy-start(f32[128,4]{0,1:T(4,128)} %param.8) | copy-start | bytes 6148
  18.5 13.4 %copy-start.3 = (bf16[128,1024]{1,0:T(8,128)(2,1)S(1)}, bf16[128,1024]{1,0:T(8,128)(2,1)}, u32[]{:S(2)}) copy-start(bf16[128,1024]{1,0:T(8,128)(2,1)} %param.11) | copy-start | bytes 786436
  18.5 61.9 %all-to-all-start = ((bf16[32,1,32,1024]{3,2,1,0:T(8,128)(2,1)}), bf16[32,1,32,1024]{3,2,1,0:T(8,128)(2,1)S(1)}, u32[]{:S(2)}, u32[]{:S(2)}) async-start(bf16[32,1,32,1024]{3,2,1,0:T(8,128)(2,1)} %bitcast.4), calls=%async_computation | async-start | bytes 4194304 | tf_op jit(solution)/shard_map/all_to_all | solution.py:84
  80.4 53.5 %copy-start.1 = (bf16[32,1,32,1024]{3,2,1,0:T(8,128)(2,1)}, bf16[32,1,32,1024]{3,2,1,0:T(8,128)(2,1)S(1)}, u32[]{:S(2)}) copy-start(bf16[32,1,32,1024]{3,2,1,0:T(8,128)(2,1)S(1)} %all-to-all-done) | copy-start | bytes 6291460
  80.4 8.0 %copy-start.4 = (bf16[1,24,1024]{2,1,0:T(8,128)(2,1)S(1)}, bf16[1,24,1024]{2,1,0:T(8,128)(2,1)}, u32[]{:S(2)}) copy-start(bf16[1,24,1024]{2,1,0:T(8,128)(2,1)} %param.10) | copy-start | bytes 147460
  80.4 58.4 %all-to-all-start.2 = ((bf16[32,1,32,1024]{3,2,1,0:T(8,128)(2,1)}), bf16[32,1,32,1024]{3,2,1,0:T(8,128)(2,1)}, u32[]{:S(2)}, u32[]{:S(2)}) async-start(bf16[32,1,32,1024]{3,2,1,0:T(8,128)(2,1)} %bitcast.21), calls=%async_computation.2 | async-start | bytes 4194304 | tf_op jit(solution)/shard_map/all_to_all | solution.py:87
  87.7 46.2 %all-gather.2.cloned.1.call-start = ((), (), s32[]{:S(2)}) async-start(), calls=%async_computation.5 | async-start | bytes 1671168 | tf_op jit(solution)/shard_map/all_gather | solution.py:81
  138.9 6.5 %copy-start.6 = (bf16[1,1024,768]{2,1,0:T(8,128)(2,1)S(1)}, bf16[1,1024,768]{2,1,0:T(8,128)(2,1)}, u32[]{:S(2)}) copy-start(bf16[1,1024,768]{2,1,0:T(8,128)(2,1)} %all-gather.2.cloned.1.call-done) | copy-start | bytes 4718596
  144.2 0.9 copy-start.7
  144.2 1.2 copy-start.9
  148.6 58.6 %all-to-all-start.3 = ((bf16[32,1,32,1024]{3,2,1,0:T(8,128)(2,1)}), bf16[32,1,32,1024]{3,2,1,0:T(8,128)(2,1)S(1)}, u32[]{:S(2)}, u32[]{:S(2)}) async-start(bf16[32,1,32,1024]{3,2,1,0:T(8,128)(2,1)} %fusion.14), calls=%async_computation.3 | async-start | bytes 4194304 | tf_op jit(solution)/shard_map/all_to_all | solution.py:89
  158.2 128.6 %all-reduce.3.cloned.1.call-start = ((), (), s32[]{:S(2)}) async-start(), calls=%async_computation.7 | async-start | bytes 3145728
  170.8 44.1 %copy-start.8 = (bf16[32,32,384]{2,1,0:T(8,128)(2,1)S(1)}, bf16[32,32,384]{2,1,0:T(8,128)(2,1)}, u32[]{:S(2)}) copy-start(bf16[32,32,384]{2,1,0:T(8,128)(2,1)} %copy-done.7) | copy-start | bytes 2359300
  207.1 150.0 %all-to-all-start.1 = ((bf16[32,1,32,1024]{3,2,1,0:T(8,128)(2,1)}), bf16[32,1,32,1024]{3,2,1,0:T(8,128)(2,1)}, u32[]{:S(2)}, u32[]{:S(2)}) async-start(bf16[32,1,32,1024]{3,2,1,0:T(8,128)(2,1)} %fusion.13), calls=%async_computation.1 | async-start | bytes 4194304 | tf_op jit(solution)/shard_map/all_to_all | solution.py:86
  214.8 135.9 %reduce-scatter.4.cloned.1.call-start = ((), (), s32[]{:S(2)}) async-start(), calls=%async_computation.6 | async-start | bytes 1671168
  219.7 2.7 copy-start.2
Sparse Core Ops, SparseCore 0:
  90.7 43.2 all-gather.1
  167.2 119.5 all-reduce.2
  289.9 60.7 reduce-scatter.3
where the time goes:
time: 372 us; the launch traced here: 371 us
  waiting for transfers between devices  229 us (62%)
  starting transfers between devices  37.9 us (10%)
  local copies, waits for them, and re-layouts  29.8 us (8%)
  matrix products  25.9 us (7%)
  blocking collectives  18.9 us (5%)
  other arithmetic  15.1 us (4%)
  between operations  14.6 us (4%)
    unnamed x5, waiting for transfers between devices  125 us
    all_to_all x1, waiting for transfers between devices, body(): lax.all_to_all(send_inputs, 'expert', split_axis=0, concat_axis=0, tiled=...  40.7 us
    all_to_all x1, waiting for transfers between devices, body(): lax.all_to_all(grad_inputs, 'expert', split_axis=0, concat_axis=0, tiled=...  36.4 us
    all_gather x1, waiting for transfers between devices, body(): lax.all_gather(w_in, 'dp', axis=1, tiled=True)  26.6 us
    all_gather x1, blocking collectives, body(): lax.all_gather(w_down, 'dp', axis=1, tiled=True)  18.9 us
    all_to_all x1, starting transfers between devices, body(): lax.all_to_all(send_inputs, 'expert', split_axis=0, concat_axis=0, tiled=...  13.2 us
    all_to_all x1, starting transfers between devices, body(): lax.all_to_all(grad_inputs, 'expert', split_axis=0, concat_axis=0, tiled=...  9.65 us
    unnamed x28, local copies, waits for them, and re-layouts  8.68 us
  transfers between devices with their start and end apart: 7, of which 5 were waited for; matrix products, arithmetic and copies ran while one was open for 11% of the time, Pallas kernels for 0%

commit v1 on v0

--- a/solution.py
+++ b/solution.py
@@ -79,7 +79,9 @@
     )
     full_in, full_down = (
         lax.all_gather(w_in, "dp", axis=1, tiled=True),
-        lax.all_gather(w_down, "dp", axis=1, tiled=True),
+        jnp.concatenate(
+            lax.all_to_all(jnp.stack([w_down] * lax.axis_size("dp")), "dp", 0, 0), axis=1
+        ),
     )
     inputs_here = lax.all_to_all(send_inputs, "expert", split_axis=0, concat_axis=0, tiled=True)
     projected_here, activation_here, results_here = expert_forward(inputs_here, full_in, full_down)

time: 372 us -> 389 us (1.046)
  waiting for transfers between devices: 229 us -> 256 us
  blocking collectives: 18.9 us -> 0 us
  starting transfers between devices: 37.9 us -> 46.3 us
    all_gather x1 -> x0, blocking collectives: 18.9 us -> none  [body(): lax.all_gather(w_down, 'dp', axis=1, tiled=True)]
    all_gather x1, waiting for transfers between devices: 26.6 us -> 43.2 us  [body(): lax.all_gather(w_in, 'dp', axis=1, tiled=True)]
    all_to_all x0 -> x1, waiting for transfers between devices: none -> 10.7 us  [body(): lax.all_to_all(jnp.stack([w_down] * lax.axis_size('dp')), 'dp', 0, 0)]
    all_to_all x0 -> x1, starting transfers between devices: none -> 9.34 us  [body(): lax.all_to_all(jnp.stack([w_down] * lax.axis_size('dp')), 'dp', 0, 0)]
    unnamed x28 -> x30, local copies, waits for them, and re-layouts: 8.68 us -> 7.96 us
  transfers between devices with their start and end apart: 7 -> 8, of which waited for: 5 -> 6; matrix products, arithmetic and copies ran while one was open for 11% -> 13% of each run, Pallas kernels for 0% -> 0%
where the time goes in v1:
time: 389 us; the launch traced here: 388 us
  waiting for transfers between devices  256 us (66%)
  starting transfers between devices  46.3 us (12%)
  local copies, waits for them, and re-layouts  30.9 us (8%)
  matrix products  25.9 us (7%)
  between operations  14.6 us (4%)
  other arithmetic  14.4 us (4%)
    unnamed x5, waiting for transfers between devices  125 us
    all_gather x1, waiting for transfers between devices, body(): lax.all_gather(w_in, 'dp', axis=1, tiled=True)  43.2 us
    all_to_all x1, waiting for transfers between devices, body(): lax.all_to_all(send_inputs, 'expert', split_axis=0, concat_axis=0, tiled=...  40.4 us
    all_to_all x1, waiting for transfers between devices, body(): lax.all_to_all(grad_inputs, 'expert', split_axis=0, concat_axis=0, tiled=...  36.2 us
    all_to_all x1, starting transfers between devices, body(): lax.all_to_all(send_inputs, 'expert', split_axis=0, concat_axis=0, tiled=...  11.5 us
    all_to_all x1, waiting for transfers between devices, body(): lax.all_to_all(jnp.stack([w_down] * lax.axis_size('dp')), 'dp', 0, 0)  10.7 us
    all_to_all x1, starting transfers between devices, body(): lax.all_to_all(grad_inputs, 'expert', split_axis=0, concat_axis=0, tiled=...  10.1 us
    all_to_all x1, starting transfers between devices, body(): lax.all_to_all(jnp.stack([w_down] * lax.axis_size('dp')), 'dp', 0, 0)  9.34 us
  transfers between devices with their start and end apart: 8, of which 6 were waited for; matrix products, arithmetic and copies ran while one was open for 13% of the time, Pallas kernels for 0%

profile of v1, /device:TPU:25, one launch (start us, length us, event | category | flops | bytes accessed | tf_op | source)
XLA Modules:
  0.0 387.9 jit_solution(11481092429921713129)
XLA Ops:
  7.2 0.0 copy-start
  7.2 0.0 copy-start.5
  7.2 1.8 stack.2
  9.0 9.3 %all-to-all-start.1 = ((bf16[16,1,24,1024]{3,2,1,0:T(8,128)(2,1)}), bf16[16,1,24,1024]{3,2,1,0:T(8,128)(2,1)S(1)}, u32[]{:S(2)}, u32[]{:S(2)}) async-start(bf16[16,1,24,1024]{3,2,1,0:T(8,128)(2,1)} %stack.2), calls=%async_computation.1 | async-start | bytes 1572864 | tf_op jit(solution)/shard_map/all_to_all | solution.py:83
  18.4 0.0 copy-done.5
  18.4 0.1 copy.34
  18.5 0.1 eq.29
  18.6 0.1 eq.25
  18.7 1.2 reduce-window.6
  19.9 0.2 slice_reduce_fusion
  20.2 0.1 copy.33
  20.3 0.1 mul.160
  20.4 0.1 fusion.49
  20.5 0.0 copy-done
  20.6 7.7 %scatter_custom_fusion = bf16[1024,1024]{1,0:T(8,128)(2,1)} fusion(s32[512]{0:T(512)S(1)} %bitcast.147, bf16[128,1024]{1,0:T(8,128)(2,1)S(1)} %copy-done, s32[1024]{0:T(1024)S(1)} %pad_clamp_fusion.1, bf16[]{:T(256)} %constant.17.clone.1), kind=kCustom, calls=%fused_computation.41 | custom fusion | bytes 2097154 | tf_op jit(solution)/shard_map/scatter | solution.py:68
  28.3 10.7 %all-to-all-done.1 = bf16[16,1,24,1024]{3,2,1,0:T(8,128)(2,1)S(1)} async-done(((bf16[16,1,24,1024]{3,2,1,0:T(8,128)(2,1)}), bf16[16,1,24,1024]{3,2,1,0:T(8,128)(2,1)S(1)}, u32[]{:S(2)}, u32[]{:S(2)}) %all-to-all-start.1) | async-done | bytes 786464 | tf_op jit(solution)/shard_map/all_to_all | solution.py:83
  39.0 11.5 %all-to-all-start = ((bf16[32,1,32,1024]{3,2,1,0:T(8,128)(2,1)}), bf16[32,1,32,1024]{3,2,1,0:T(8,128)(2,1)S(1)}, u32[]{:S(2)}, u32[]{:S(2)}) async-start(bf16[32,1,32,1024]{3,2,1,0:T(8,128)(2,1)} %bitcast.4), calls=%async_computation | async-start | bytes 4194304 | tf_op jit(solution)/shard_map/all_to_all | solution.py:86
  50.5 0.0 copy-done.6
  50.5 0.1 copy.38
  50.6 0.1 mul.173
  50.7 0.0 copy-done.3
  50.7 7.8 %scatter_custom_fusion.1 = bf16[1024,1024]{1,0:T(8,128)(2,1)} fusion(s32[512]{0:T(512)S(1)} %bitcast.148, f32[512]{0:T(512)S(1)} %mul.173, bf16[]{:T(256)} %constant.17.clone.1, bf16[128,1024]{1,0:T(8,128)(2,1)S(1)} %copy-done.3, s32[1024]{0:T(1024)S(1)} %pad_clamp_fusion.1), kind=kCustom, calls=%fused_computation.40 | custom fusion | flops 1572864 | bytes 2365442 | tf_op jit(solution)/shard_map/scatter | solution.py:77
  58.5 40.4 %all-to-all-done = bf16[32,1,32,1024]{3,2,1,0:T(8,128)(2,1)S(1)} async-done(((bf16[32,1,32,1024]{3,2,1,0:T(8,128)(2,1)}), bf16[32,1,32,1024]{3,2,1,0:T(8,128)(2,1)S(1)}, u32[]{:S(2)}, u32[]{:S(2)}) %all-to-all-start) | async-done | bytes 2097184 | tf_op jit(solution)/shard_map/all_to_all | solution.py:86
  98.9 7.6 %all-to-all-start.3 = ((bf16[32,1,32,1024]{3,2,1,0:T(8,128)(2,1)}), bf16[32,1,32,1024]{3,2,1,0:T(8,128)(2,1)}, u32[]{:S(2)}, u32[]{:S(2)}) async-start(bf16[32,1,32,1024]{3,2,1,0:T(8,128)(2,1)} %bitcast.22), calls=%async_computation.3 | async-start | bytes 4194304 | tf_op jit(solution)/shard_map/all_to_all | solution.py:89
  106.5 0.0 all-gather.2.cloned.1.call-start
  106.6 0.7 all-gather.2.cloned.1.call-update
  107.3 43.2 %all-gather.2.cloned.1.call-done = bf16[1,1024,768]{2,1,0:T(8,128)(2,1)} async-done(((bf16[1,64,768]{2,1,0:T(8,128)(2,1)}), bf16[1,1024,768]{2,1,0:T(8,128)(2,1)}) %all-gather.2.cloned.1.call-update) | async-done | bytes 1572880 | tf_op jit(solution)/shard_map/all_gather | solution.py:81
  150.5 0.0 copy-done.1
  150.5 4.9 %multiply_bitcast_fusion = f32[32,1,32,768]{3,2,0,1:T(8,128)} fusion(bf16[32,1,32,1024]{3,2,1,0:T(8,128)(2,1)S(1)} %all-to-all-done, bf16[1,1024,768]{2,1,0:T(8,128)(2,1)} %all-gather.2.cloned.1.call-done), kind=kOutput, calls=%fused_computation.10 | convolution fusion | flops 1611399168 | bytes 6815744 | tf_op jit(solution)/shard_map/sxcd,xdj->sxcj/dot_general | solution.py:22
  155.4 0.0 all-to-all-done.3
  155.4 5.4 %fusion.42 = (bf16[32,32,384]{2,1,0:T(8,128)(2,1)S(1)}, bf16[32,32,384]{2,1,0:T(8,128)(2,1)S(1)}, bf16[32,32,384]{2,1,0:T(8,128)(2,1)}) fusion(f32[32,1,32,768]{3,2,0,1:T(8,128)} %multiply_bitcast_fusion, bf16[384,1024,1]{1,0,2:T(8,128)(2,1)S(1)} %bitcast.144, bf16[32,1,32,1024]{3,2,1,0:T(8,128)(2,1)} %all-to-all-done.3), kind=kOutput, calls=%fused_computation.48 | convolution fusion | flops 811597824 | bytes 8388608 | tf_op jit(solution)/shard_map/sxcd,xfd->sxcf/dot_general | solution.py:38
  160.8 0.9 copy-done.8
  161.7 0.3 copy-done.10
  161.9 0.0 copy-done.7
  161.9 3.2 fusion.14
  165.1 10.1 %all-to-all-start.4 = ((bf16[32,1,32,1024]{3,2,1,0:T(8,128)(2,1)}), bf16[32,1,32,1024]{3,2,1,0:T(8,128)(2,1)S(1)}, u32[]{:S(2)}, u32[]{:S(2)}) async-start(bf16[32,1,32,1024]{3,2,1,0:T(8,128)(2,1)} %fusion.14), calls=%async_computation.4 | async-start | bytes 4194304 | tf_op jit(solution)/shard_map/all_to_all | solution.py:91
  175.2 0.0 all-reduce.3.cloned.1.call-start
  175.3 3.9 %fusion.31 = bf16[384,1,1024]{0,2,1:T(8,128)(2,1)} fusion(bf16[32,32,384]{2,1,0:T(8,128)(2,1)} %get-tuple-element.18, bf16[32,1,32,1024]{3,2,1,0:T(8,128)(2,1)} %all-to-all-done.3), kind=kOutput, calls=%fused_computation.39 | convolution fusion | flops 806092800 | bytes 3670016 | tf_op jit(solution)/shard_map/sxcf,sxcd->fxd/dot_general | solution.py:114
  179.2 4.8 %copy.43 = bf16[384,1,1024]{2,1,0:T(2,128)(2,1)} copy(bf16[384,1,1024]{0,2,1:T(8,128)(2,1)} %fusion.31) | data formatting | bytes 1572864 | tf_op jit(solution)/shard_map/convert_element_type | solution.py:116
  184.0 0.0 all-reduce.3.cloned.1.call-update
  184.0 3.7 fusion.13
  187.7 36.2 %all-to-all-done.4 = bf16[32,1,32,1024]{3,2,1,0:T(8,128)(2,1)S(1)} async-done(((bf16[32,1,32,1024]{3,2,1,0:T(8,128)(2,1)}), bf16[32,1,32,1024]{3,2,1,0:T(8,128)(2,1)S(1)}, u32[]{:S(2)}, u32[]{:S(2)}) %all-to-all-start.4) | async-done | bytes 2097184 | tf_op jit(solution)/shard_map/all_to_all | solution.py:91
  223.9 7.6 %all-to-all-start.2 = ((bf16[32,1,32,1024]{3,2,1,0:T(8,128)(2,1)}), bf16[32,1,32,1024]{3,2,1,0:T(8,128)(2,1)}, u32[]{:S(2)}, u32[]{:S(2)}) async-start(bf16[32,1,32,1024]{3,2,1,0:T(8,128)(2,1)} %fusion.13), calls=%async_computation.2 | async-start | bytes 4194304 | tf_op jit(solution)/shard_map/all_to_all | solution.py:88
  231.5 0.0 reduce-scatter.4.cloned.1.call-start
  231.6 0.0 copy-done.9
  231.6 4.8 %fusion.23 = bf16[1024,768]{0,1:T(8,128)(2,1)} fusion(bf16[32,1,32,1024]{3,2,1,0:T(8,128)(2,1)} %copy-done.1, bf16[32,32,384]{2,1,0:T(8,128)(2,1)} %copy-done.10, bf16[32,32,384]{2,1,0:T(8,128)(2,1)S(1)} %copy-done.9), kind=kOutput, calls=%fused_computation.37 | convolution fusion | flops 1615331328 | bytes 5242880 | tf_op jit(solution)/shard_map/sxcd,sxcj->dxj/dot_general | solution.py:102
  236.5 2.6 copy.48
  239.1 0.0 reduce-scatter.4.cloned.1.call-update
  239.1 0.2 copy.41
  239.3 1.3 dynamic-slice
  241.2 62.4 %all-reduce.3.cloned.1.call-done = bf16[384,1,1024]{2,1,0:T(2,128)(2,1)} async-done(((bf16[384,1,1024]{2,1,0:T(2,128)(2,1)}), bf16[384,1,1024]{2,1,0:T(2,128)(2,1)}) %all-reduce.3.cloned.1.call-update) | async-done | bytes 786448
  303.6 1.0 fusion.47
  304.6 0.6 copy.45
  305.3 62.2 %reduce-scatter.4.cloned.1.call-done = bf16[64,768]{1,0:T(8,128)(2,1)} async-done(((bf16[1024,768]{1,0:T(8,128)(2,1)}), bf16[64,768]{1,0:T(8,128)(2,1)}) %reduce-scatter.4.cloned.1.call-update) | async-done | bytes 98320
  367.5 1.1 copy.49
  368.5 0.1 fusion.43
  368.6 0.8 copy.44
  369.4 2.0 gather_fusion.1
  371.4 0.4 gather.18
  371.9 2.1 reduce_sum.32
  374.0 0.0 all-to-all-done.2
  374.0 4.6 %gather_fusion = bf16[512,1024]{1,0:T(8,128)(2,1)S(1)} fusion(bf16[1024,1024]{1,0:T(8,128)(2,1)} %bitcast.21, s32[1024]{0:T(1024)S(1)} %pad_clamp_fusion), kind=kCustom, calls=%fused_computation.1 | custom fusion | bytes 2099200 | tf_op jit(solution)/shard_map/gather | solution.py:92
  378.6 0.7 reshape.225
  379.3 2.1 multiply_reduce_fusion
  (20 shorter events, 0.1 us)
Async XLA Ops:
  7.2 13.4 %copy-start = (bf16[128,1024]{1,0:T(8,128)(2,1)S(1)}, bf16[128,1024]{1,0:T(8,128)(2,1)}, u32[]{:S(2)}) copy-start(bf16[128,1024]{1,0:T(8,128)(2,1)} %param.6) | copy-start | bytes 786436
  7.2 11.2 %copy-start.5 = (s32[128,4]{0,1:T(4,128)S(1)}, s32[128,4]{0,1:T(4,128)}, u32[]{:S(2)}) copy-start(s32[128,4]{0,1:T(4,128)} %param.7) | copy-start | bytes 6148
  9.0 29.9 %all-to-all-start.1 = ((bf16[16,1,24,1024]{3,2,1,0:T(8,128)(2,1)}), bf16[16,1,24,1024]{3,2,1,0:T(8,128)(2,1)S(1)}, u32[]{:S(2)}, u32[]{:S(2)}) async-start(bf16[16,1,24,1024]{3,2,1,0:T(8,128)(2,1)} %stack.2), calls=%async_computation.1 | async-start | bytes 1572864 | tf_op jit(solution)/shard_map/all_to_all | solution.py:83
  39.0 11.5 %copy-start.6 = (f32[128,4]{0,1:T(4,128)S(1)}, f32[128,4]{0,1:T(4,128)}, u32[]{:S(2)}) copy-start(f32[128,4]{0,1:T(4,128)} %param.8) | copy-start | bytes 6148
  39.0 11.7 %copy-start.3 = (bf16[128,1024]{1,0:T(8,128)(2,1)S(1)}, bf16[128,1024]{1,0:T(8,128)(2,1)}, u32[]{:S(2)}) copy-start(bf16[128,1024]{1,0:T(8,128)(2,1)} %param.11) | copy-start | bytes 786436
  39.0 59.9 %all-to-all-start = ((bf16[32,1,32,1024]{3,2,1,0:T(8,128)(2,1)}), bf16[32,1,32,1024]{3,2,1,0:T(8,128)(2,1)S(1)}, u32[]{:S(2)}, u32[]{:S(2)}) async-start(bf16[32,1,32,1024]{3,2,1,0:T(8,128)(2,1)} %bitcast.4), calls=%async_computation | async-start | bytes 4194304 | tf_op jit(solution)/shard_map/all_to_all | solution.py:86
  98.9 51.6 %copy-start.1 = (bf16[32,1,32,1024]{3,2,1,0:T(8,128)(2,1)}, bf16[32,1,32,1024]{3,2,1,0:T(8,128)(2,1)S(1)}, u32[]{:S(2)}) copy-start(bf16[32,1,32,1024]{3,2,1,0:T(8,128)(2,1)S(1)} %all-to-all-done) | copy-start | bytes 6291460
  98.9 56.5 %all-to-all-start.3 = ((bf16[32,1,32,1024]{3,2,1,0:T(8,128)(2,1)}), bf16[32,1,32,1024]{3,2,1,0:T(8,128)(2,1)}, u32[]{:S(2)}, u32[]{:S(2)}) async-start(bf16[32,1,32,1024]{3,2,1,0:T(8,128)(2,1)} %bitcast.22), calls=%async_computation.3 | async-start | bytes 4194304 | tf_op jit(solution)/shard_map/all_to_all | solution.py:89
  106.5 43.9 %all-gather.2.cloned.1.call-start = ((), (), s32[]{:S(2)}) async-start(), calls=%async_computation.6 | async-start | bytes 1671168 | tf_op jit(solution)/shard_map/all_gather | solution.py:81
  155.4 6.5 %copy-start.7 = (bf16[1,1024,768]{2,1,0:T(8,128)(2,1)S(1)}, bf16[1,1024,768]{2,1,0:T(8,128)(2,1)}, u32[]{:S(2)}) copy-start(bf16[1,1024,768]{2,1,0:T(8,128)(2,1)} %all-gather.2.cloned.1.call-done) | copy-start | bytes 4718596
  160.8 0.9 copy-start.8
  160.8 1.2 copy-start.10
  165.1 58.8 %all-to-all-start.4 = ((bf16[32,1,32,1024]{3,2,1,0:T(8,128)(2,1)}), bf16[32,1,32,1024]{3,2,1,0:T(8,128)(2,1)S(1)}, u32[]{:S(2)}, u32[]{:S(2)}) async-start(bf16[32,1,32,1024]{3,2,1,0:T(8,128)(2,1)} %fusion.14), calls=%async_computation.4 | async-start | bytes 4194304 | tf_op jit(solution)/shard_map/all_to_all | solution.py:91
  175.2 128.4 %all-reduce.3.cloned.1.call-start = ((), (), s32[]{:S(2)}) async-start(), calls=%async_computation.8 | async-start | bytes 3145728
  187.7 43.9 %copy-start.9 = (bf16[32,32,384]{2,1,0:T(8,128)(2,1)S(1)}, bf16[32,32,384]{2,1,0:T(8,128)(2,1)}, u32[]{:S(2)}) copy-start(bf16[32,32,384]{2,1,0:T(8,128)(2,1)} %copy-done.8) | copy-start | bytes 2359300
  223.9 150.1 %all-to-all-start.2 = ((bf16[32,1,32,1024]{3,2,1,0:T(8,128)(2,1)}), bf16[32,1,32,1024]{3,2,1,0:T(8,128)(2,1)}, u32[]{:S(2)}, u32[]{:S(2)}) async-start(bf16[32,1,32,1024]{3,2,1,0:T(8,128)(2,1)} %fusion.13), calls=%async_computation.2 | async-start | bytes 4194304 | tf_op jit(solution)/shard_map/all_to_all | solution.py:88
  231.5 135.9 %reduce-scatter.4.cloned.1.call-start = ((), (), s32[]{:S(2)}) async-start(), calls=%async_computation.7 | async-start | bytes 1671168
  236.5 2.7 copy-start.2
  236.5 67.2 %copy-start.4 = (bf16[1,24,1024]{2,1,0:T(8,128)(2,1)S(1)}, bf16[1,24,1024]{2,1,0:T(8,128)(2,1)}, u32[]{:S(2)}) copy-start(bf16[1,24,1024]{2,1,0:T(8,128)(2,1)} %param.10) | copy-start | bytes 147460
Sparse Core Ops, SparseCore 0:
  109.5 40.9 all-gather.1
  184.2 119.4 all-reduce.2
  306.7 60.7 reduce-scatter.3
